TPU v7x, 256 devices: a whole 4x4x8 slice. The times are simulated.
256 devices in a mesh: dp: 8 (over y, core), mp: 32 (over z, x).
Axes of the slice: x: 4, y: 4, z: 8, core: 2. Of those that a mesh axis runs over, the one named last changes fastest.
Arguments:
- table: bfloat16 [32, 2048, 128], P('mp'), may hold values from -6 to 6
- ids: int32 [65536, 32, 2], P('dp', 'mp'), may hold values from 0 to 2047
- counts: int32 [256, 8], P(('dp', 'mp')), may hold values from 1 to 96, 256 in all within a row
- labels: int32 [65536], P(('dp', 'mp')), may hold values from 0 to 4
- request_home: int32 [2048], replicated, may hold values from 0 to 2047, each once
- user_codes: bfloat16 [2048, 1024], P('dp'), may hold values from -6 to 6
- cross_down: bfloat16 [4096, 256], replicated, may hold values from -0.09375 to 0.09375
- cross_up: bfloat16 [256, 4096], replicated, may hold values from -0.375 to 0.375
- cross_bias: float32 [4096], replicated, may hold values from -4 to 4
- tower_weight: bfloat16 [4096, 1024], P('mp'), may hold values from -0.09375 to 0.09375
- tower_bias: float32 [1024], replicated, may hold values from -3 to 3
Outputs:
- scores: float32 [65536], P(('dp', 'mp'))
- pooled_grad: bfloat16 [65536, 32, 128], P('dp', 'mp')
Inputs may be any that keep to these rules, and one draw needn't show every extreme that they name: `counts`: each row sums to 256; its largest entry is exactly 96. `request_home`: a permutation of the request slots.
All inputs are finite; a program needn't handle non-finite values.
Results may differ from a plain program's by a relative error of at most 0.0097.
Values may be sent and summed in bfloat16 or wider, within the bound.
No kernel may reach another device: no remote copies, remote signals or barrier semaphores. Data moves between devices by JAX's collectives and lax.ppermute only.
A program may use at most 128 MiB of HBM per device.

v0:
```python
import jax
import jax.numpy as jnp
from jax import lax
from jax.sharding import PartitionSpec as P


def members(counts_row, rows):
    ends = jnp.cumsum(counts_row)
    starts = ends - counts_row
    place = jnp.arange(rows, dtype=jnp.int32)[:, None]
    return (place >= starts[None, :]) & (place < ends[None, :])


def dot_last(left, right):
    return lax.dot_general(
        left, right, (((1,), (1,)), ((), ())), preferred_element_type=jnp.float32
    )


def pair_grad(scores, member, labels):
    gain = jnp.exp2(labels.astype(jnp.float32))
    member_f = member.astype(jnp.float32)
    same = jnp.dot(member_f, member_f.T) > 0.5
    diff = gain[:, None] - gain[None, :]
    gap = scores[None, :] - scores[:, None]
    turn = jnp.where(diff > 0, jax.nn.sigmoid(gap), jax.nn.sigmoid(-gap))
    total = jnp.sum(jnp.where(same, diff * turn, 0.0), axis=1)
    seg_gain = jnp.sum(jnp.where(member, (gain - 1.0)[:, None], 0.0), axis=0)
    norm = jnp.sum(jnp.where(member, seg_gain[None, :], 0.0), axis=1)
    return -total / jnp.maximum(norm, 1.0)


def local(
    table,
    ids,
    counts,
    labels,
    request_home,
    user_codes,
    cross_down,
    cross_up,
    cross_bias,
    tower_weight,
    tower_bias,
):
    f32, bf16 = (jnp.float32, jnp.bfloat16)
    n_mp = lax.axis_size("mp")
    n_dp = lax.axis_size("dp")
    d_idx = lax.axis_index("dp")
    m_idx = lax.axis_index("mp")
    rows = labels.shape[0]
    seg_count = counts.shape[1]
    width = user_codes.shape[1]
    emb = table.shape[2]
    rank = cross_down.shape[1]
    scale = 1.0 / jnp.sqrt(jnp.float32(width))
    piece = tower_weight.shape[1] // n_dp
    w_piece = lax.dynamic_slice_in_dim(tower_weight, d_idx * piece, piece, axis=1)
    w_cols = lax.all_gather(w_piece, "mp", axis=0, tiled=True)
    w_all = lax.all_gather(w_cols, "dp", axis=1, tiled=True)
    w3 = w_all.reshape(n_mp, emb, width)
    held = user_codes.shape[0]
    home_local = lax.dynamic_slice_in_dim(request_home, d_idx * held, held)
    wanted = (
        (jnp.arange(n_dp, dtype=jnp.int32)[:, None] * n_mp + m_idx) * seg_count
        + jnp.arange(seg_count, dtype=jnp.int32)[None, :]
    ).reshape(-1)
    pick = (home_local[None, :] == wanted[:, None]).astype(bf16)
    mine = jnp.dot(pick, user_codes, preferred_element_type=f32).astype(bf16)
    user_seg = lax.psum_scatter(
        mine.reshape(n_dp, seg_count, width), "dp", scatter_dimension=0, tiled=False
    )
    slab = table[0]
    picked = jnp.take(slab, ids[:, 0, :], axis=0, mode="clip")
    pooled = jnp.sum(picked.astype(f32), axis=1).astype(bf16)
    x0f = lax.all_to_all(
        pooled.reshape(n_mp, rows, emb), "mp", split_axis=0, concat_axis=0, tiled=True
    )
    member = members(counts[0], rows)
    cd3 = cross_down.reshape(n_mp, emb, rank)
    cu3 = cross_up.reshape(rank, n_mp, emb)
    bias3 = cross_bias.reshape(n_mp, 1, emb)
    z = jnp.einsum("fcd,fdr->cr", x0f, cd3, preferred_element_type=f32).astype(bf16)
    cross = jnp.einsum("cr,rfd->fcd", z, cu3, preferred_element_type=f32) + bias3
    x1 = (x0f * cross + x0f).astype(bf16)
    act = jnp.einsum("fcd,fdh->ch", x1, w3, preferred_element_type=f32) + tower_bias
    sig = jax.nn.sigmoid(act)
    hidden = (act * sig).astype(bf16)
    pair = dot_last(hidden, user_seg)
    score = jnp.sum(jnp.where(member, pair, 0.0), axis=1) * scale
    dscore = pair_grad(score, member, labels)
    code = jnp.dot(member.astype(bf16), user_seg, preferred_element_type=f32)
    slope = sig * (1.0 + act * (1.0 - sig))
    dact = (dscore[:, None] * code * scale * slope).astype(bf16)
    dx1 = jnp.einsum("ch,fdh->fcd", dact, w3, preferred_element_type=f32)
    dcross = (dx1 * x0f).astype(bf16)
    dz = jnp.einsum("fcd,rfd->cr", dcross, cu3, preferred_element_type=f32).astype(bf16)
    dx0 = dx1 * (1.0 + cross) + jnp.einsum("cr,fdr->fcd", dz, cd3, preferred_element_type=f32)
    grads = dx0.astype(bf16)
    returned = lax.all_to_all(grads, "mp", split_axis=0, concat_axis=0, tiled=True)
    return (score, returned.reshape(n_mp * rows, 1, emb))


def solution(mesh):
    in_specs = (
        P("mp", None, None),
        P("dp", "mp", None),
        P(("dp", "mp"), None),
        P(("dp", "mp")),
        P(),
        P("dp", None),
        P(),
        P(),
        P(),
        P("mp", None),
        P(),
    )
    out_specs = (P(("dp", "mp")), P("dp", "mp", None))
    return jax.shard_map(local, mesh=mesh, in_specs=in_specs, out_specs=out_specs, check_vma=False)
```

profile of v0, /device:TPU:10, one launch (start us, length us, event | category | flops | bytes accessed | tf_op | source)
XLA Modules:
  0.0 346.3 jit_solution(14947742715400940034)
XLA Ops:
  7.2 0.0 copy-start
  7.2 0.0 all-gather.3.cloned.1.call-start
  7.2 1.5 constant_dynamic-slice_fusion
  8.7 0.0 all-gather.3.cloned.1.call-update
  8.8 0.0 all-gather.5.cloned.1.call-start
  8.8 80.5 %all-gather.3.cloned.1.call-done = bf16[4096,128]{1,0:T(8,128)(2,1)} async-done(((bf16[128,128]{1,0:T(8,128)(2,1)}), bf16[4096,128]{1,0:T(8,128)(2,1)}) %all-gather.3.cloned.1.call-update) | async-done | bytes 1048592 | tf_op jit(solution)/shard_map/all_gather | solution.py:59
  89.3 0.0 all-gather.5.cloned.1.call-update
  89.3 3.4 copy.18
  92.7 0.0 copy-start.1
  92.7 4.1 %reshape.87 = s32[16384]{0:T(1024)S(1)} reshape(s32[8192,1,2]{2,0,1:T(8,128)} %copy.18) | data formatting | bytes 131072 | tf_op jit(solution)/shard_map/jit(_take)/broadcast_in_dim | solution.py:74
  96.8 0.0 copy-done.1
  96.8 57.8 %gather_fusion = bf16[16384,128]{1,0:T(8,128)(2,1)} fusion(bf16[2048,128]{1,0:T(8,128)(2,1)S(1)} %bitcast.114, s32[16384]{0:T(1024)S(1)} %broadcast_clamp_fusion), kind=kCustom, calls=%fused_computation | custom fusion | bytes 8454144 | tf_op jit(solution)/shard_map/jit(_take)/gather | solution.py:74
  154.6 45.8 %reduce_sum.48 = bf16[8192,128]{1,0:T(8,128)(2,1)} reduce(bf16[8192,2,128]{2,1,0:T(2,128)(2,1)} %bitcast.115, bf16[]{:T(256)} %constant.18.clone.1), dimensions={1}, to_apply=%region_1.2 | reduce | flops 1048576 | bytes 6291458 | tf_op jit(solution)/shard_map/reduce_sum | solution.py:75
  200.4 0.0 copy-start.2
  200.5 0.0 copy-start.8
  200.5 0.0 copy-start.4
  200.5 7.7 %all-to-all-start = ((bf16[32,256,128]{2,1,0:T(8,128)(2,1)}), bf16[32,256,128]{2,1,0:T(8,128)(2,1)}, u32[]{:S(2)}, u32[]{:S(2)}) async-start(bf16[32,256,128]{2,1,0:T(8,128)(2,1)} %bitcast.116), calls=%async_computation | async-start | bytes 4194304 | tf_op jit(solution)/shard_map/all_to_all | solution.py:76
  208.1 0.2 reduce-scatter.2.cloned.1.call-start
  208.4 0.1 iota_add_fusion
  208.4 0.1 add.100
  208.5 0.8 dynamic_slice.7
  209.3 0.0 copy-done.2
  209.3 0.9 fusion.36
  210.2 0.0 reduce-scatter.2.cloned.1.call-update
  210.2 0.0 copy-done.8
  210.2 0.2 reduce-window.4
  210.4 0.0 copy-done.4
  210.4 0.2 select_reduce_fusion.1
  210.6 0.1 select_reduce_fusion
  210.7 42.6 %all-to-all-done = bf16[32,256,128]{2,1,0:T(8,128)(2,1)} async-done(((bf16[32,256,128]{2,1,0:T(8,128)(2,1)}), bf16[32,256,128]{2,1,0:T(8,128)(2,1)}, u32[]{:S(2)}, u32[]{:S(2)}) %all-to-all-start) | async-done | bytes 2097184 | tf_op jit(solution)/shard_map/all_to_all | solution.py:76
  253.3 0.0 copy-done
  253.3 0.0 copy-start.3
  253.3 0.0 copy-start.7
  253.3 6.6 %fusion.8 = f32[256,32,128]{2,0,1:T(8,128)} fusion(bf16[32,256,128]{2,1,0:T(8,128)(2,1)} %all-to-all-done, bf16[32,128,256]{2,1,0:T(8,128)(2,1)S(1)} %bitcast.112, bf16[256,4096]{1,0:T(8,128)(2,1)} %param.18), kind=kOutput, calls=%fused_computation.12 | convolution fusion | flops 1073807360 | bytes 10485760 | tf_op jit(solution)/shard_map/cr,rfd->fcd/dot_general | solution.py:84
  259.9 0.0 all-gather.5.cloned.1.call-done
  259.9 0.0 copy-done.3
  259.9 0.0 copy-done.7
  259.9 6.7 %fusion.18 = f32[256,1024]{1,0:T(8,128)S(1)} fusion(bf16[32,128,1024]{2,1,0:T(8,128)(2,1)} %bitcast.125, bf16[32,256,128]{2,1,0:T(8,128)(2,1)} %all-to-all-done, f32[256,32,128]{2,0,1:T(8,128)} %fusion.8, f32[32,128]{1,0:T(8,128)S(1)} %bitcast.118, f32[1024]{0:T(1024)S(1)} %copy-done.7), kind=kOutput, calls=%fused_computation.21 | convolution fusion | flops 2152988672 | bytes 15749120 | tf_op jit(solution)/shard_map/fcd,fdh->ch/dot_general | solution.py:86
  266.6 0.0 reduce-scatter.2.cloned.1.call-done
  266.6 1.1 fusion.47
  267.8 0.0 copy-start.6
  267.8 0.0 copy-start.5
  267.8 0.4 fusion.35
  268.2 0.3 copy-done.6
  268.5 7.1 %fusion.48 = f32[32,128,256]{1,2,0:T(8,128)} fusion(bf16[32,128,1024]{2,1,0:T(8,128)(2,1)} %bitcast.126, f32[256,1024]{1,0:T(8,128)S(1)} %fusion.18, f32[256]{0:T(256)S(1)} %maximum_divide_fusion, bf16[1,8,1024]{2,1,0:T(8,128)(2,1)S(1)} %copy-done.6, s32[8]{0:T(128)S(1)} %bitcast.124, s32[8]{0:T(128)S(1)} %fusion.65), kind=kOutput, calls=%fused_computation.39 | convolution fusion | flops 2154567680 | bytes 13648960 | tf_op jit(solution)/shard_map/ch,fdh->fcd/dot_general | solution.py:95
  275.6 0.0 copy-done.5
  275.6 9.6 %fusion.2 = bf16[32,256,128]{2,1,0:T(8,128)(2,1)} fusion(f32[32,128,256]{1,2,0:T(8,128)} %fusion.48, f32[256,32,128]{2,0,1:T(8,128)} %fusion.8, bf16[32,128,256]{2,1,0:T(8,128)(2,1)S(1)} %bitcast.113, f32[32,128]{1,0:T(8,128)S(1)} %bitcast.119, bf16[32,256,128]{2,1,0:T(8,128)(2,1)} %all-to-all-done, bf16[256,4096]{1,0:T(8,128)(2,1)} %param.18), kind=kOutput, calls=%fused_computation.6 | convolution fusion | flops 1082195968 | bytes 16793600 | tf_op jit(solution)/shard_map/cr,fdr->fcd/dot_general | solution.py:98
  285.2 53.3 %all_to_all.10 = bf16[32,256,128]{2,1,0:T(8,128)(2,1)S(1)} all-to-all(bf16[32,256,128]{2,1,0:T(8,128)(2,1)} %fusion.2), channel_id=1, replica_groups=mesh['dp'=8,'mp'=32] {'mp'}, dimensions={0} | all-to-all | bytes 4194304 | tf_op jit(solution)/shard_map/all_to_all | solution.py:100
  338.4 1.3 copy.43
  (6 shorter events, 0.0 us)
Async XLA Ops:
  7.2 246.1 %copy-start = (bf16[4096,256]{1,0:T(8,128)(2,1)S(1)}, bf16[4096,256]{1,0:T(8,128)(2,1)}, u32[]{:S(2)}) copy-start(bf16[4096,256]{1,0:T(8,128)(2,1)} %param.17) | copy-start | bytes 6291460
  7.2 82.1 %all-gather.3.cloned.1.call-start = ((), (), s32[]{:S(2)}) async-start(), calls=%async_computation.3 | async-start | bytes 1081344 | tf_op jit(solution)/shard_map/all_gather | solution.py:59
  8.8 251.1 %all-gather.5.cloned.1.call-start = ((), (), s32[]{:S(2)}) async-start(), calls=%async_computation.4 | async-start | bytes 9437184 | tf_op jit(solution)/shard_map/all_gather | solution.py:60
  92.7 4.1 %copy-start.1 = (bf16[1,2048,128]{2,1,0:T(8,128)(2,1)S(1)}, bf16[1,2048,128]{2,1,0:T(8,128)(2,1)}, u32[]{:S(2)}) copy-start(bf16[1,2048,128]{2,1,0:T(8,128)(2,1)} %param.11) | copy-start | bytes 1572868
  200.4 8.8 %copy-start.2 = (bf16[256,1024]{1,0:T(8,128)(2,1)S(1)}, bf16[256,1024]{1,0:T(8,128)(2,1)}, u32[]{:S(2)}) copy-start(bf16[256,1024]{1,0:T(8,128)(2,1)} %param.16) | copy-start | bytes 1572868
  200.5 9.8 %copy-start.8 = (s32[1,8]{1,0:T(1,128)S(1)}, s32[1,8]{1,0:T(1,128)}, u32[]{:S(2)}) copy-start(s32[1,8]{1,0:T(1,128)} %param.13) | copy-start | bytes 100
  200.5 10.0 %copy-start.4 = (s32[256]{0:T(256)S(1)}, s32[256]{0:T(256)}, u32[]{:S(2)}) copy-start(s32[256]{0:T(256)} %param.14) | copy-start | bytes 3076
  200.5 52.8 %all-to-all-start = ((bf16[32,256,128]{2,1,0:T(8,128)(2,1)}), bf16[32,256,128]{2,1,0:T(8,128)(2,1)}, u32[]{:S(2)}, u32[]{:S(2)}) async-start(bf16[32,256,128]{2,1,0:T(8,128)(2,1)} %bitcast.116), calls=%async_computation | async-start | bytes 4194304 | tf_op jit(solution)/shard_map/all_to_all | solution.py:76
  208.1 58.5 %reduce-scatter.2.cloned.1.call-start = ((), (), s32[]{:S(2)}) async-start(), calls=%async_computation.5 | async-start | bytes 147456 | tf_op jit(solution)/shard_map/reduce_scatter | solution.py:70
  253.3 6.6 %copy-start.3 = (f32[4096]{0:T(1024)S(1)}, f32[4096]{0:T(1024)}, u32[]{:S(2)}) copy-start(f32[4096]{0:T(1024)} %param.19) | copy-start | bytes 49156
  253.3 6.6 %copy-start.7 = (f32[1024]{0:T(1024)S(1)}, f32[1024]{0:T(1024)}, u32[]{:S(2)}) copy-start(f32[1024]{0:T(1024)} %param.21) | copy-start | bytes 12292
  267.8 0.7 copy-start.6
  267.8 7.8 %copy-start.5 = (f32[256]{0:T(256)}, f32[256]{0:T(256)S(1)}, u32[]{:S(2)}) copy-start(f32[256]{0:T(256)S(1)} %broadcast_multiply_fusion) | copy-start | bytes 3076
Sparse Core Ops, SparseCore 0:
  11.1 78.0 all-gather.2
  91.1 54.5 all-gather.4
  211.4 31.8 reduce-scatter.1
where the time goes:
time: 347 us; the launch traced here: 346 us
  waiting for transfers between devices  123 us (35%)
  local copies, waits for them, and re-layouts  69.3 us (20%)
  blocking collectives  53.3 us (15%)
  other arithmetic  46.4 us (13%)
  matrix products  32.4 us (9%)
  between operations  13.9 us (4%)
  starting transfers between devices  7.95 us (2%)
    all_gather x1, waiting for transfers between devices, local(): w_cols = lax.all_gather(w_piece, 'mp', axis=0, tiled=True)  80.5 us
    gather x1, local copies, waits for them, and re-layouts, local(): picked = jnp.take(slab, ids[:, 0, :], axis=0, mode='clip')  57.8 us
    all_to_all x1, blocking collectives, local(): lax.all_to_all(grads, 'mp', split_axis=0, concat_axis=0, tiled=True)  53.3 us
    reduce_sum x1, other arithmetic, local(): pooled = jnp.sum(picked.astype(f32), axis=1).astype(bf16)  45.8 us
    all_to_all x1, waiting for transfers between devices, local(): lax.all_to_all(pooled.reshape(n_mp, rows, emb), 'mp', split_axis=0, conca...  42.6 us
    dot_general x1, matrix products, local(): jnp.einsum('cr,fdr->fcd', dz, cd3, preferred_element_type=f32)  9.56 us
    all_to_all x1, starting transfers between devices, local(): lax.all_to_all(pooled.reshape(n_mp, rows, emb), 'mp', split_axis=0, conca...  7.65 us
    dot_general x1, matrix products, local(): dx1 = jnp.einsum('ch,fdh->fcd', dact, w3, preferred_element_type=f32)  7.13 us
  transfers between devices with their start and end apart: 4, of which 2 were waited for; matrix products, arithmetic and copies ran while one was open for 37% of the time, Pallas kernels for 0%

commit v1 on v0

--- a/solution.py
+++ b/solution.py
@@ -57,7 +57,21 @@
     piece = tower_weight.shape[1] // n_dp
     w_piece = lax.dynamic_slice_in_dim(tower_weight, d_idx * piece, piece, axis=1)
     w_cols = lax.all_gather(w_piece, "mp", axis=0, tiled=True)
-    w_all = lax.all_gather(w_cols, "dp", axis=1, tiled=True)
+    ways, here, turn_2 = (lax.axis_size("dp"), lax.axis_index("dp"), w_cols.shape[1])
+    dims = [n * ways if d == 1 else n for d, n in enumerate(w_cols.shape)]
+    full = lax.dynamic_update_slice_in_dim(
+        jnp.zeros(dims, w_cols.dtype), w_cols, here * turn_2, axis=1
+    )
+    going_up = going_down = w_cols
+    for far in range(1, ways // 2 + 1):
+        going_up = lax.ppermute(going_up, "dp", [(d, (d + 1) % ways) for d in range(ways)])
+        full = lax.dynamic_update_slice_in_dim(full, going_up, (here - far) % ways * turn_2, axis=1)
+        if 2 * far < ways:
+            going_down = lax.ppermute(going_down, "dp", [(d, (d - 1) % ways) for d in range(ways)])
+            full = lax.dynamic_update_slice_in_dim(
+                full, going_down, (here + far) % ways * turn_2, axis=1
+            )
+    w_all = full
     w3 = w_all.reshape(n_mp, emb, width)
     held = user_codes.shape[0]
     home_local = lax.dynamic_slice_in_dim(request_home, d_idx * held, held)

time: 347 us -> 298 us (0.86)
  waiting for transfers between devices: 123 us -> 42.1 us
  local copies, waits for them, and re-layouts: 69.3 us -> 85.7 us
  starting transfers between devices: 7.95 us -> 15.9 us
  blocking collectives: 53.3 us -> 56.8 us
    all_gather x1, waiting for transfers between devices: 80.5 us -> 0.02 us  [local(): w_cols = lax.all_gather(w_piece, 'mp', axis=0, tiled=True)]
    all_to_all x1, waiting for transfers between devices: 42.6 us -> 17.6 us  [local(): lax.all_to_all(pooled.reshape(n_mp, rows, emb), 'mp', split_axis=0, conca...]
    ppermute x0 -> x7, waiting for transfers between devices: none -> 24.5 us  [the longest x4 18.4 us: local(): lax.ppermute(going_up, 'dp', [(d, (d + 1) % ways) for d in range(ways)])]
    dynamic_update_slice x0 -> x8, local copies, waits for them, and re-layouts: none -> 12.9 us  [the longest x3 6.01 us: local(): lax.dynamic_update_slice_in_dim(full, going_down, (here + far) % ways * t...]
    broadcast_in_dim x0 -> x1, local copies, waits for them, and re-layouts: none -> 4.3 us  [local(): jnp.zeros(dims, w_cols.dtype)]
    all_to_all x1, starting transfers between devices: 7.65 us -> 11.7 us  [local(): lax.all_to_all(pooled.reshape(n_mp, rows, emb), 'mp', split_axis=0, conca...]
    ppermute x0 -> x7, starting transfers between devices: none -> 3.98 us  [the longest x3 3.44 us: local(): lax.ppermute(going_down, 'dp', [(d, (d - 1) % ways) for d in range(ways)])]
    all_to_all x1, blocking collectives: 53.3 us -> 56.8 us  [local(): lax.all_to_all(grads, 'mp', split_axis=0, concat_axis=0, tiled=True)]
  transfers between devices with their start and end apart: 4 -> 10, of which waited for: 2 -> 5; matrix products, arithmetic and copies ran while one was open for 37% -> 49% of each run, Pallas kernels for 0% -> 0%
where the time goes in v1:
time: 298 us
  local copies, waits for them, and re-layouts  85.7 us (29%)
  blocking collectives  56.8 us (19%)
  other arithmetic  46.4 us (16%)
  waiting for transfers between devices  42.1 us (14%)
  matrix products  34.9 us (12%)
  starting transfers between devices  15.9 us (5%)
  between operations  15.8 us (5%)
    gather x1, local copies, waits for them, and re-layouts, local(): picked = jnp.take(slab, ids[:, 0, :], axis=0, mode='clip')  57.4 us
    all_to_all x1, blocking collectives, local(): lax.all_to_all(grads, 'mp', split_axis=0, concat_axis=0, tiled=True)  56.8 us
    reduce_sum x1, other arithmetic, local(): pooled = jnp.sum(picked.astype(f32), axis=1).astype(bf16)  45.8 us
    ppermute x4, waiting for transfers between devices, local(): lax.ppermute(going_up, 'dp', [(d, (d + 1) % ways) for d in range(ways)])  18.4 us
    all_to_all x1, waiting for transfers between devices, local(): lax.all_to_all(pooled.reshape(n_mp, rows, emb), 'mp', split_axis=0, conca...  17.6 us
    all_to_all x1, starting transfers between devices, local(): lax.all_to_all(pooled.reshape(n_mp, rows, emb), 'mp', split_axis=0, conca...  11.7 us
    dot_general x1, matrix products, local(): jnp.einsum('cr,fdr->fcd', dz, cd3, preferred_element_type=f32)  9.56 us
    dot_general x1, matrix products, local(): jnp.einsum('fcd,fdh->ch', x1, w3, preferred_element_type=f32) + tower_bias  7.44 us
  transfers between devices with their start and end apart: 10, of which 5 were waited for; matrix products, arithmetic and copies ran while one was open for 49% of the time, Pallas kernels for 0%

profile of v1, /device:TPU:10, one launch (start us, length us, event | category | flops | bytes accessed | tf_op | source)
XLA Modules:
  0.0 297.6 jit_solution(11523332863614143359)
XLA Ops:
  8.0 0.0 copy-start
  8.0 0.0 all-gather.2.cloned.1.call-start
  8.1 1.5 constant_dynamic-slice_fusion
  9.6 0.0 all-gather.2.cloned.1.call-update
  9.6 0.0 copy-start.1
  9.6 3.4 %copy.18 = s32[8192,1,2]{2,0,1:T(8,128)} copy(s32[8192,1,2]{0,2,1:T(2,128)} %param.12) | data formatting | bytes 131072 | tf_op args[1]
  13.0 4.0 %reshape.87 = s32[16384]{0:T(1024)S(1)} reshape(s32[8192,1,2]{2,0,1:T(8,128)} %copy.18) | data formatting | bytes 131072 | tf_op jit(solution)/shard_map/jit(_take)/broadcast_in_dim | solution.py:88
  17.0 0.0 copy-done.1
  17.1 57.4 %gather_fusion = bf16[16384,128]{1,0:T(8,128)(2,1)} fusion(bf16[2048,128]{1,0:T(8,128)(2,1)S(1)} %bitcast.114, s32[16384]{0:T(1024)S(1)} %broadcast_clamp_fusion), kind=kCustom, calls=%fused_computation | custom fusion | bytes 8454144 | tf_op jit(solution)/shard_map/jit(_take)/gather | solution.py:88
  74.4 0.0 copy-start.5
  74.4 45.8 %reduce_sum.48 = bf16[8192,128]{1,0:T(8,128)(2,1)} reduce(bf16[8192,2,128]{2,1,0:T(2,128)(2,1)} %bitcast.115, bf16[]{:T(256)} %constant.72.clone.1), dimensions={1}, to_apply=%region_1.2 | reduce | flops 1048576 | bytes 6291458 | tf_op jit(solution)/shard_map/reduce_sum | solution.py:89
  120.3 11.7 %all-to-all-start = ((bf16[32,256,128]{2,1,0:T(8,128)(2,1)}), bf16[32,256,128]{2,1,0:T(8,128)(2,1)}, u32[]{:S(2)}, u32[]{:S(2)}) async-start(bf16[32,256,128]{2,1,0:T(8,128)(2,1)} %bitcast.116), calls=%async_computation | async-start | bytes 4194304 | tf_op jit(solution)/shard_map/all_to_all | solution.py:90
  132.0 0.2 reduce-scatter.2.cloned.1.call-start
  132.2 0.0 all-gather.2.cloned.1.call-done
  132.2 0.0 collective-permute-start
  132.3 0.1 iota_add_fusion
  132.3 0.1 add.174
  132.4 0.8 dynamic_slice.7
  133.2 1.9 fusion.36
  135.1 0.0 reduce-scatter.2.cloned.1.call-update
  135.3 0.0 copy-done.9
  135.3 0.2 reduce-window.4
  135.5 1.7 collective-permute-start.1
  137.2 0.0 copy-done.5
  137.2 0.2 select_reduce_fusion.1
  137.4 9.3 %collective-permute-done = bf16[4096,128]{1,0:T(8,128)(2,1)S(1)} collective-permute-done((bf16[4096,128]{1,0:T(8,128)(2,1)}, bf16[4096,128]{1,0:T(8,128)(2,1)S(1)}, u32[]{:S(2)}, u32[]{:S(2)}) %collective-permute-start) | collective-permute-done | bytes 1048608 | tf_op jit(solution)/shard_map/ppermute | solution.py:67
  146.7 0.0 collective-permute-start.2
  146.7 0.1 select_reduce_fusion
  146.8 4.3 %broadcast_in_dim.29 = bf16[4096,1024]{1,0:T(8,128)(2,1)} broadcast(bf16[]{:T(256)} %constant.72.clone.1), dimensions={} | broadcast | bytes 8388610 | tf_op jit(solution)/shard_map/broadcast_in_dim | solution.py:63
  151.1 0.0 copy-done.3
  151.1 1.2 constant_dynamic-update-slice_fusion.7
  152.2 0.0 collective-permute-done.1
  152.2 1.7 collective-permute-start.3
  154.0 1.1 constant_dynamic-update-slice_fusion.6
  155.1 6.2 %collective-permute-done.2 = bf16[4096,128]{1,0:T(8,128)(2,1)} collective-permute-done((bf16[4096,128]{1,0:T(8,128)(2,1)S(1)}, bf16[4096,128]{1,0:T(8,128)(2,1)}, u32[]{:S(2)}, u32[]{:S(2)}) %collective-permute-start.2) | collective-permute-done | bytes 1048608 | tf_op jit(solution)/shard_map/ppermute | solution.py:67
  161.3 0.0 collective-permute-start.4
  161.3 2.3 constant_dynamic-update-slice_fusion.5
  163.7 17.6 %all-to-all-done = bf16[32,256,128]{2,1,0:T(8,128)(2,1)} async-done(((bf16[32,256,128]{2,1,0:T(8,128)(2,1)}), bf16[32,256,128]{2,1,0:T(8,128)(2,1)}, u32[]{:S(2)}, u32[]{:S(2)}) %all-to-all-start) | async-done | bytes 2097184 | tf_op jit(solution)/shard_map/all_to_all | solution.py:90
  181.3 0.0 copy-done
  181.3 6.5 %fusion.8 = f32[256,32,128]{2,0,1:T(8,128)} fusion(bf16[32,256,128]{2,1,0:T(8,128)(2,1)} %all-to-all-done, bf16[32,128,256]{2,1,0:T(8,128)(2,1)S(1)} %bitcast.112, bf16[256,4096]{1,0:T(8,128)(2,1)} %param.18), kind=kOutput, calls=%fused_computation.12 | convolution fusion | flops 1073807360 | bytes 10485760 | tf_op jit(solution)/shard_map/cr,rfd->fcd/dot_general | solution.py:98
  187.8 0.0 collective-permute-done.3
  187.8 0.0 collective-permute-start.5
  187.8 2.4 constant_dynamic-update-slice_fusion.4
  190.2 0.0 collective-permute-done.4
  190.2 0.5 collective-permute-start.6
  190.7 2.6 constant_dynamic-update-slice_fusion.3
  193.3 1.1 constant_dynamic-update-slice_fusion.2
  194.4 6.1 %collective-permute-done.5 = bf16[4096,128]{1,0:T(8,128)(2,1)S(1)} collective-permute-done((bf16[4096,128]{1,0:T(8,128)(2,1)}, bf16[4096,128]{1,0:T(8,128)(2,1)S(1)}, u32[]{:S(2)}, u32[]{:S(2)}) %collective-permute-start.5) | collective-permute-done | bytes 1048608 | tf_op jit(solution)/shard_map/ppermute | solution.py:70
  200.4 1.1 constant_dynamic-update-slice_fusion.1
  201.6 2.9 collective-permute-done.6
  204.4 1.1 constant_dynamic-update-slice_fusion
  205.5 0.0 copy-done.2
  205.5 0.0 copy-done.4
  205.5 0.0 copy-done.8
  205.5 7.4 %fusion.18 = f32[256,1024]{1,0:T(8,128)} fusion(bf16[32,128,1024]{2,1,0:T(8,128)(2,1)} %bitcast.12, bf16[32,256,128]{2,1,0:T(8,128)(2,1)} %all-to-all-done, f32[256,32,128]{2,0,1:T(8,128)S(1)} %copy-done.2, f32[32,128]{1,0:T(8,128)S(1)} %bitcast.118, f32[1024]{0:T(1024)S(1)} %copy-done.8), kind=kOutput, calls=%fused_computation.21 | convolution fusion | flops 2152988672 | bytes 15749120 | tf_op jit(solution)/shard_map/fcd,fdh->ch/dot_general | solution.py:100
  213.0 1.6 fusion.47
  214.6 0.0 copy-start.6
  214.7 0.4 fusion.35
  215.1 0.0 copy-done.7
  215.1 7.4 %fusion.48 = f32[32,128,256]{1,2,0:T(8,128)} fusion(bf16[32,128,1024]{2,1,0:T(8,128)(2,1)} %bitcast.12, f32[256,1024]{1,0:T(8,128)} %fusion.18, f32[256]{0:T(256)S(1)} %maximum_divide_fusion, bf16[1,8,1024]{2,1,0:T(8,128)(2,1)S(1)} %copy-done.7, s32[8]{0:T(128)S(1)} %bitcast.124, s32[8]{0:T(128)S(1)} %fusion.65), kind=kOutput, calls=%fused_computation.39 | convolution fusion | flops 2154567680 | bytes 13648960 | tf_op jit(solution)/shard_map/ch,fdh->fcd/dot_general | solution.py:109
  222.4 0.0 copy-done.6
  222.5 9.6 %fusion.2 = bf16[32,256,128]{2,1,0:T(8,128)(2,1)} fusion(f32[32,128,256]{1,2,0:T(8,128)} %fusion.48, f32[256,32,128]{2,0,1:T(8,128)} %fusion.8, bf16[32,128,256]{2,1,0:T(8,128)(2,1)S(1)} %bitcast.113, f32[32,128]{1,0:T(8,128)S(1)} %bitcast.119, bf16[32,256,128]{2,1,0:T(8,128)(2,1)} %all-to-all-done, bf16[256,4096]{1,0:T(8,128)(2,1)} %param.18), kind=kOutput, calls=%fused_computation.6 | convolution fusion | flops 1082195968 | bytes 16793600 | tf_op jit(solution)/shard_map/cr,fdr->fcd/dot_general | solution.py:112
  232.0 56.8 %all_to_all.10 = bf16[32,256,128]{2,1,0:T(8,128)(2,1)S(1)} all-to-all(bf16[32,256,128]{2,1,0:T(8,128)(2,1)} %fusion.2), channel_id=1, replica_groups=mesh['dp'=8,'mp'=32] {'mp'}, dimensions={0} | all-to-all | bytes 4194304 | tf_op jit(solution)/shard_map/all_to_all | solution.py:114
  288.8 1.3 copy.51
  (13 shorter events, 0.0 us)
Async XLA Ops:
  8.0 173.3 %copy-start = (bf16[4096,256]{1,0:T(8,128)(2,1)S(1)}, bf16[4096,256]{1,0:T(8,128)(2,1)}, u32[]{:S(2)}) copy-start(bf16[4096,256]{1,0:T(8,128)(2,1)} %param.17) | copy-start | bytes 6291460
  8.0 124.2 %all-gather.2.cloned.1.call-start = ((), (), s32[]{:S(2)}) async-start(), calls=%async_computation.3 | async-start | bytes 1081344 | tf_op jit(solution)/shard_map/all_gather | solution.py:59
  9.6 7.5 %copy-start.1 = (bf16[1,2048,128]{2,1,0:T(8,128)(2,1)S(1)}, bf16[1,2048,128]{2,1,0:T(8,128)(2,1)}, u32[]{:S(2)}) copy-start(bf16[1,2048,128]{2,1,0:T(8,128)(2,1)} %param.11) | copy-start | bytes 1572868
  74.4 60.8 %copy-start.9 = (s32[1,8]{1,0:T(1,128)S(1)}, s32[1,8]{1,0:T(1,128)}, u32[]{:S(2)}) copy-start(s32[1,8]{1,0:T(1,128)} %param.13) | copy-start | bytes 100
  74.4 62.7 %copy-start.5 = (s32[256]{0:T(256)S(1)}, s32[256]{0:T(256)}, u32[]{:S(2)}) copy-start(s32[256]{0:T(256)} %param.14) | copy-start | bytes 3076
  120.3 61.0 %all-to-all-start = ((bf16[32,256,128]{2,1,0:T(8,128)(2,1)}), bf16[32,256,128]{2,1,0:T(8,128)(2,1)}, u32[]{:S(2)}, u32[]{:S(2)}) async-start(bf16[32,256,128]{2,1,0:T(8,128)(2,1)} %bitcast.116), calls=%async_computation | async-start | bytes 4194304 | tf_op jit(solution)/shard_map/all_to_all | solution.py:90
  132.0 81.0 %reduce-scatter.2.cloned.1.call-start = ((), (), s32[]{:S(2)}) async-start(), calls=%async_computation.4 | async-start | bytes 147456 | tf_op jit(solution)/shard_map/reduce_scatter | solution.py:84
  132.2 14.4 %collective-permute-start = (bf16[4096,128]{1,0:T(8,128)(2,1)}, bf16[4096,128]{1,0:T(8,128)(2,1)S(1)}, u32[]{:S(2)}, u32[]{:S(2)}) collective-permute-start(bf16[4096,128]{1,0:T(8,128)(2,1)} %all-gather.2.cloned.1.call-done), channel_id=1, source_target_pairs={{0,32},{32,64},{64,96},{96,128},{128,160},{160,192},{192,224},{224... | collective-permute-start | bytes 3145736 | tf_op jit(solution)/shard_map/ppermute | solution.py:67
  135.5 16.8 %collective-permute-start.1 = (bf16[4096,128]{1,0:T(8,128)(2,1)}, bf16[4096,128]{1,0:T(8,128)(2,1)}, u32[]{:S(2)}, u32[]{:S(2)}) collective-permute-start(bf16[4096,128]{1,0:T(8,128)(2,1)} %all-gather.2.cloned.1.call-done), channel_id=1, source_target_pairs={{0,224},{32,0},{64,32},{96,64},{128,96},{160,128},{192,160},{224,1... | collective-permute-start | bytes 3145736 | tf_op jit(solution)/shard_map/ppermute | solution.py:70
  146.7 14.7 %collective-permute-start.2 = (bf16[4096,128]{1,0:T(8,128)(2,1)S(1)}, bf16[4096,128]{1,0:T(8,128)(2,1)}, u32[]{:S(2)}, u32[]{:S(2)}) collective-permute-start(bf16[4096,128]{1,0:T(8,128)(2,1)S(1)} %collective-permute-done), channel_id=1, source_target_pairs={{0,32},{32,64},{64,96},{96,128},{128,160},{160,192},{192,224},{224... | collective-permute-start | bytes 3145736 | tf_op jit(solution)/shard_map/ppermute | solution.py:67
  146.8 4.3 %copy-start.3 = (bf16[4096,128]{1,0:T(8,128)(2,1)S(1)}, bf16[4096,128]{1,0:T(8,128)(2,1)}, u32[]{:S(2)}) copy-start(bf16[4096,128]{1,0:T(8,128)(2,1)} %all-gather.2.cloned.1.call-done) | copy-start | bytes 3145732
  152.2 35.6 %collective-permute-start.3 = (bf16[4096,128]{1,0:T(8,128)(2,1)}, bf16[4096,128]{1,0:T(8,128)(2,1)}, u32[]{:S(2)}, u32[]{:S(2)}) collective-permute-start(bf16[4096,128]{1,0:T(8,128)(2,1)} %collective-permute-done.1), channel_id=1, source_target_pairs={{0,224},{32,0},{64,32},{96,64},{128,96},{160,128},{192,160},{224,1... | collective-permute-start | bytes 3145736 | tf_op jit(solution)/shard_map/ppermute | solution.py:70
  161.3 28.9 %collective-permute-start.4 = (bf16[4096,128]{1,0:T(8,128)(2,1)}, bf16[4096,128]{1,0:T(8,128)(2,1)S(1)}, u32[]{:S(2)}, u32[]{:S(2)}) collective-permute-start(bf16[4096,128]{1,0:T(8,128)(2,1)} %collective-permute-done.2), channel_id=1, source_target_pairs={{0,32},{32,64},{64,96},{96,128},{128,160},{160,192},{192,224},{224... | collective-permute-start | bytes 3145736 | tf_op jit(solution)/shard_map/ppermute | solution.py:67
  187.8 12.6 %collective-permute-start.5 = (bf16[4096,128]{1,0:T(8,128)(2,1)}, bf16[4096,128]{1,0:T(8,128)(2,1)S(1)}, u32[]{:S(2)}, u32[]{:S(2)}) collective-permute-start(bf16[4096,128]{1,0:T(8,128)(2,1)} %collective-permute-done.3), channel_id=1, source_target_pairs={{0,224},{32,0},{64,32},{96,64},{128,96},{160,128},{192,160},{224,1... | collective-permute-start | bytes 3145736 | tf_op jit(solution)/shard_map/ppermute | solution.py:70
  190.2 15.3 %copy-start.2 = (f32[256,32,128]{2,0,1:T(8,128)S(1)}, f32[256,32,128]{2,0,1:T(8,128)}, u32[]{:S(2)}) copy-start(f32[256,32,128]{2,0,1:T(8,128)} %fusion.8) | copy-start | bytes 12582916
  190.2 15.3 %copy-start.4 = (f32[4096]{0:T(1024)S(1)}, f32[4096]{0:T(1024)}, u32[]{:S(2)}) copy-start(f32[4096]{0:T(1024)} %param.19) | copy-start | bytes 49156
  190.2 15.3 %copy-start.8 = (f32[1024]{0:T(1024)S(1)}, f32[1024]{0:T(1024)}, u32[]{:S(2)}) copy-start(f32[1024]{0:T(1024)} %param.21) | copy-start | bytes 12292
  190.2 14.2 %collective-permute-start.6 = (bf16[4096,128]{1,0:T(8,128)(2,1)S(1)}, bf16[4096,128]{1,0:T(8,128)(2,1)S(1)}, u32[]{:S(2)}, u32[]{:S(2)}) collective-permute-start(bf16[4096,128]{1,0:T(8,128)(2,1)S(1)} %collective-permute-done.4), channel_id=1, source_target_pairs={{0,32},{32,64},{64,96},{96,128},{128,160},{160,192},{192,224},{224... | collective-permute-start | bytes 3145736 | tf_op jit(solution)/shard_map/ppermute | solution.py:67
  213.0 2.1 copy-start.7
  214.6 7.8 %copy-start.6 = (f32[256]{0:T(256)}, f32[256]{0:T(256)S(1)}, u32[]{:S(2)}) copy-start(f32[256]{0:T(256)S(1)} %broadcast_multiply_fusion) | copy-start | bytes 3076
Sparse Core Ops, SparseCore 0:
  11.4 78.0 all-gather.1
Sparse Core Ops, SparseCore 1:
  135.2 32.9 reduce-scatter.1
